TPU v7x, 512 devices: a whole 4x4x16 slice. The times are simulated.
512 devices in a mesh: lat: 32 (over z, core), lon: 16 (over x, y).
Axes of the slice: x: 4, y: 4, z: 16, core: 2. Of those that a mesh axis runs over, the one named last changes fastest.
Arguments:
- source: float32 [8, 1024, 2048], P(None, 'lat', 'lon'), may hold values from -6 to 6
- kappa_lon: bfloat16 [8, 1024, 2048], P(None, 'lat', 'lon'), may hold values from 32768 to 262144
- kappa_lat: bfloat16 [8, 1024, 2048], P(None, 'lat', 'lon'), may hold values from 2048 to 16384
- sea_mask: int32 [8, 1024, 2048], P(None, 'lat', 'lon'), may hold values 0 or 1
Outputs:
- analysis: float32 [8, 1024, 2048], P(None, 'lat', 'lon')
All inputs are finite; a program needn't handle non-finite values. No bound on the sum of `sea_mask` on one device may be relied on, other than what follows from the above.
Results may differ from a plain program's by a relative error of at most 0.0003.
Values sent between devices are 32-bit elements; how exact they have to be, the bound alone decides.
No kernel may reach another device: no remote copies, remote signals or barrier semaphores. Data moves between devices by JAX's collectives and lax.ppermute only.
A program may use at most 64 MiB of HBM per device.

v0:
```python
import jax
import jax.numpy as jnp
from jax import lax
from jax.sharding import PartitionSpec as P


def earlier(values, stride, axis):
    length = values.shape[axis]
    padding = jnp.zeros_like(lax.slice_in_dim(values, 0, stride, axis=axis))
    return jnp.concatenate([padding, lax.slice_in_dim(values, 0, length - stride, axis=axis)], axis)


def following(values, stride, axis):
    length = values.shape[axis]
    padding = jnp.zeros_like(lax.slice_in_dim(values, 0, stride, axis=axis))
    return jnp.concatenate([lax.slice_in_dim(values, stride, length, axis=axis), padding], axis)


def local_solve(lower_band, upper_band, excess, sources, axis):
    length = lower_band.shape[axis]
    stride = 1
    while stride < length:
        inverse = 1.0 / (excess - lower_band - upper_band)
        left_weight = -lower_band * earlier(inverse, stride, axis)
        right_coefficient = -upper_band * following(inverse, stride, axis)
        new_lower = left_weight * earlier(lower_band, stride, axis)
        new_upper = right_coefficient * following(upper_band, stride, axis)
        excess = (
            excess
            + left_weight * earlier(excess, stride, axis)
            + right_coefficient * following(excess, stride, axis)
        )
        sources = (
            sources
            + left_weight * earlier(sources, stride, axis + 1)
            + right_coefficient * following(sources, stride, axis + 1)
        )
        lower_band, upper_band = (new_lower, new_upper)
        stride = stride * 2
    return sources / (excess - lower_band - upper_band)


def circular_solve(lower_band, upper_band, excess, sources):
    devices = lower_band.shape[0]
    stride = 1
    while stride < devices:
        inverse = 1.0 / (excess - lower_band - upper_band)
        left_weight = -lower_band * jnp.roll(inverse, stride, 0)
        right_coefficient = -upper_band * jnp.roll(inverse, -stride, 0)
        new_lower = left_weight * jnp.roll(lower_band, stride, 0)
        new_upper = right_coefficient * jnp.roll(upper_band, -stride, 0)
        excess = (
            excess
            + left_weight * jnp.roll(excess, stride, 0)
            + right_coefficient * jnp.roll(excess, -stride, 0)
        )
        sources = (
            sources
            + left_weight * jnp.roll(sources, stride, 0)
            + right_coefficient * jnp.roll(sources, -stride, 0)
        )
        lower_band, upper_band = (new_lower, new_upper)
        stride = stride * 2
    return sources / excess


def line_pass(values, faces, edge_kappa, edge_wet, axis, mesh_axis, periodic):
    length = values.shape[axis]
    position = lax.broadcasted_iota(jnp.int32, values.shape, axis)
    zero = jnp.zeros_like(lax.slice_in_dim(values, 0, 1, axis=axis))
    left_face = jnp.concatenate([zero, faces], axis)
    right_face = jnp.concatenate([faces, zero], axis)
    sources = jnp.stack(
        [values, jnp.where(position == 0, 1.0, 0.0), jnp.where(position == length - 1, 1.0, 0.0)], 0
    )
    solved = local_solve(-left_face, -right_face, jnp.ones_like(values), sources, axis)
    particular, from_left, from_right = (solved[0], solved[1], solved[2])

    def row_at(member, place):
        return lax.index_in_dim(member, place, axis, keepdims=False)

    terms = jnp.stack(
        [
            row_at(particular, 0),
            row_at(from_left, 0),
            row_at(from_right, 0),
            row_at(particular, length - 1),
            row_at(from_left, length - 1),
            row_at(from_right, length - 1),
            edge_kappa,
            edge_wet,
        ],
        0,
    )
    gathered = lax.all_gather(terms[None], mesh_axis, axis=0, tiled=True)
    head_p, head_u, head_w, tail_p, tail_u, tail_w, tail_kappa, head_wet = (
        gathered[:, k] for k in range(terms.shape[0])
    )
    devices = gathered.shape[0]

    def next_of(member):
        return jnp.roll(member, -1, 0)

    face = tail_kappa * next_of(head_wet)
    if not periodic:
        device = lax.broadcasted_iota(jnp.int32, face.shape, 0)
        face = jnp.where(device == devices - 1, 0.0, face)
    lower = -face * tail_u
    upper = -face * next_of(head_w)
    diagonal = 1.0 + face * (next_of(head_u) + tail_w)
    flux = circular_solve(lower, upper, diagonal + lower + upper, face * (next_of(head_p) - tail_p))
    index = lax.axis_index(mesh_axis)
    here = lax.dynamic_index_in_dim(flux, index, 0, keepdims=False)
    before = lax.dynamic_index_in_dim(flux, (index + devices - 1) % devices, 0, keepdims=False)
    return (
        particular
        - from_left * jnp.expand_dims(before, axis)
        + from_right * jnp.expand_dims(here, axis)
    )


def shards(source, kappa_lon, kappa_lat, sea_mask):
    wet_cells = sea_mask.astype(jnp.float32)
    lon_kappa = kappa_lon.astype(jnp.float32)
    lat_kappa = kappa_lat.astype(jnp.float32)
    lon_weight = lon_kappa * wet_cells
    lat_weight = lat_kappa * wet_cells
    lon_faces = lon_weight[:, :, :-1] * wet_cells[:, :, 1:]
    lon_pass = line_pass(
        source, lon_faces, lon_weight[:, :, -1], wet_cells[:, :, 0], 2, "lon", True
    )
    lat_faces = lat_weight[:, :-1, :] * wet_cells[:, 1:, :]
    lat_pass = line_pass(
        lon_pass, lat_faces, lat_weight[:, -1, :], wet_cells[:, 0, :], 1, "lat", False
    )
    return wet_cells * 4.0 * jnp.sqrt(jnp.sqrt(lon_kappa * lat_kappa)) * lat_pass


def solution(mesh):
    return jax.shard_map(
        shards,
        mesh=mesh,
        in_specs=(
            P(None, "lat", "lon"),
            P(None, "lat", "lon"),
            P(None, "lat", "lon"),
            P(None, "lat", "lon"),
        ),
        out_specs=P(None, "lat", "lon"),
        check_vma=False,
    )
```

profile of v0, /device:TPU:1, one launch (start us, length us, event | category | flops | bytes accessed | tf_op | source)
XLA Modules:
  0.0 180.2 jit_solution(14112881031736275784)
XLA Ops:
  7.6 1.0 copy.506
  8.6 1.0 copy.505
  9.6 1.2 copy.504
  10.9 0.9 convert_multiply_fusion
  11.9 1.1 slice_negate_fusion.2
  13.0 0.9 subtract_divide_fusion.11
  13.9 0.8 pad_maximum_fusion.1
  14.7 1.5 copy.508
  16.5 0.8 copy-done.2
  17.4 0.9 copy-done.9
  25.7 0.7 constant_dynamic-update-slice_fusion.1
  26.4 20.1 %all-gather = f32[128,8,32]{2,1,0:T(8,128)S(1)} all-gather(f32[8,8,32]{2,1,0:T(8,128)S(1)} %constant_dynamic-update-slice_fusion), channel_id=2, replica_groups=mesh['lat'=32,'lon'=16] {'lon'}, dimensions={0}, use_global_device_ids=true | all-gather | bytes 139264 | tf_op jit(solution)/shard_map/all_gather | solution.py:95
  47.0 0.6 slice.1325
  47.6 0.6 slice.1320
  48.3 0.6 slice.1319
  48.9 0.6 fusion.139
  49.5 0.7 fusion.140
  50.1 0.6 fusion.137
  50.7 0.6 fusion.138
  51.5 0.7 fusion.130
  52.2 0.6 fusion.131
  52.8 1.2 slice_multiply_fusion
  54.2 1.3 slice_negate_fusion
  55.5 1.0 subtract_divide_fusion.4
  56.5 1.0 slice.1382
  57.7 0.7 fusion.136
  58.5 0.6 fusion.128
  59.1 1.1 add_divide_fusion.3
  61.8 0.8 copy-done.7
  63.6 0.6 multiply_add_fusion.3
  72.3 0.8 add_divide_fusion
  73.0 0.9 slice_bitcast_fusion
  73.9 1.1 fusion.78
  75.1 1.2 copy.517
  76.3 2.4 %fusion.77 = (f32[8,1,128]{1,0,2:T(8,128)}, f32[8,1,128]{1,0,2:T(8,128)}) fusion(f32[8,32,128]{1,0,2:T(8,128)} %get-tuple-element.112), kind=kLoop, calls=%fused_computation.294 | loop fusion | bytes 16384 | tf_op jit(solution)/shard_map/slice | solution.py:80
  78.7 1.2 copy.518
  79.9 1.1 fusion.76
  81.0 1.3 copy.519
  82.3 1.2 copy.520
  83.5 1.2 copy.521
  84.8 1.2 copy.522
  86.5 0.6 copy-done.38
  87.2 78.7 %all-gather.4.cloned.1.call-done = f32[256,8,128]{2,1,0:T(8,128)} async-done(((f32[8,8,128]{2,1,0:T(8,128)}), f32[256,8,128]{2,1,0:T(8,128)}) %all-gather.4.cloned.1.call-update) | async-done | bytes 1048592 | tf_op jit(solution)/shard_map/all_gather | solution.py:95
  165.9 0.7 slice_bitcast_fusion.22
  166.6 1.1 slice_bitcast_fusion.10
  167.7 1.1 fusion.11
  168.8 1.0 subtract_divide_fusion.16
  172.5 0.9 copy.532
  (270 shorter events, 22.5 us)
Async XLA Ops:
  6.5 159.3 %all-gather.4.cloned.1.call-start = ((), (), s32[]{:S(2)}) async-start(), calls=%async_computation | async-start | bytes 1081344 | tf_op jit(solution)/shard_map/all_gather | solution.py:95
  9.6 2.2 %copy-start.3 = (bf16[8,32,128]{1,0,2:T(8,128)(2,1)}, bf16[8,32,128]{1,0,2:T(8,128)(2,1)S(1)}, u32[]{:S(2)}) copy-start(bf16[8,32,128]{1,0,2:T(8,128)(2,1)S(1)} %copy.505) | copy-start | bytes 196612
  11.8 2.0 %copy-start.5 = (f32[8,32,128]{1,0,2:T(8,128)}, f32[8,32,128]{1,0,2:T(8,128)S(1)}, u32[]{:S(2)}) copy-start(f32[8,32,128]{1,0,2:T(8,128)S(1)} %get-tuple-element.176) | copy-start | bytes 393220
  11.9 2.0 %copy-start.31 = (f32[8,32,128]{2,1,0:T(8,128)S(1)}, f32[8,32,128]{2,1,0:T(8,128)}, u32[]{:S(2)}) copy-start(f32[8,32,128]{2,1,0:T(8,128)} %param.4) | copy-start | bytes 393220
  16.2 1.0 copy-start.2
  16.3 1.2 copy-start.19
  17.3 1.1 copy-start.9
  17.3 1.2 copy-start.10
  17.3 1.4 copy-start.18
  47.0 5.8 %copy-start.14 = (f32[16,8,32]{2,1,0:T(8,128)}, f32[16,8,32]{2,1,0:T(8,128)S(1)}, u32[]{:S(2)}) copy-start(f32[16,8,32]{2,1,0:T(8,128)S(1)} %get-tuple-element.61) | copy-start | bytes 49156
  47.0 5.8 %copy-start.16 = (f32[16,8,32]{2,1,0:T(8,128)}, f32[16,8,32]{2,1,0:T(8,128)S(1)}, u32[]{:S(2)}) copy-start(f32[16,8,32]{2,1,0:T(8,128)S(1)} %get-tuple-element.62) | copy-start | bytes 49156
  54.0 2.5 %copy-start = (f32[8,32,128]{1,0,2:T(8,128)S(1)}, f32[8,32,128]{1,0,2:T(8,128)}, u32[]{:S(2)}) copy-start(f32[8,32,128]{1,0,2:T(8,128)} %get-tuple-element.175) | copy-start | bytes 393220
  54.1 3.5 %copy-start.15 = (f32[16,8,32]{2,1,0:T(8,128)S(1)}, f32[16,8,32]{2,1,0:T(8,128)}, u32[]{:S(2)}) copy-start(f32[16,8,32]{2,1,0:T(8,128)} %copy-done.14) | copy-start | bytes 49156
  54.1 3.5 %copy-start.17 = (f32[16,8,32]{2,1,0:T(8,128)S(1)}, f32[16,8,32]{2,1,0:T(8,128)}, u32[]{:S(2)}) copy-start(f32[16,8,32]{2,1,0:T(8,128)} %copy-done.16) | copy-start | bytes 49156
  54.1 3.5 %copy-start.22 = (f32[12,8,32]{2,1,0:T(8,128)S(1)}, f32[12,8,32]{2,1,0:T(8,128)}, u32[]{:S(2)}) copy-start(f32[12,8,32]{2,1,0:T(8,128)} %slice.1325) | copy-start | bytes 36868
  54.1 3.5 %copy-start.23 = (f32[12,8,32]{2,1,0:T(8,128)S(1)}, f32[12,8,32]{2,1,0:T(8,128)}, u32[]{:S(2)}) copy-start(f32[12,8,32]{2,1,0:T(8,128)} %slice.1320) | copy-start | bytes 36868
  54.1 3.5 %copy-start.26 = (f32[12,8,32]{2,1,0:T(8,128)S(1)}, f32[12,8,32]{2,1,0:T(8,128)}, u32[]{:S(2)}) copy-start(f32[12,8,32]{2,1,0:T(8,128)} %get-tuple-element.295) | copy-start | bytes 36868
  54.1 3.5 %copy-start.27 = (f32[12,8,32]{2,1,0:T(8,128)S(1)}, f32[12,8,32]{2,1,0:T(8,128)}, u32[]{:S(2)}) copy-start(f32[12,8,32]{2,1,0:T(8,128)} %get-tuple-element.296) | copy-start | bytes 36868
  54.1 3.5 %copy-start.28 = (f32[12,8,32]{2,1,0:T(8,128)S(1)}, f32[12,8,32]{2,1,0:T(8,128)}, u32[]{:S(2)}) copy-start(f32[12,8,32]{2,1,0:T(8,128)} %get-tuple-element.291) | copy-start | bytes 36868
  54.1 3.5 %copy-start.29 = (f32[12,8,32]{2,1,0:T(8,128)S(1)}, f32[12,8,32]{2,1,0:T(8,128)}, u32[]{:S(2)}) copy-start(f32[12,8,32]{2,1,0:T(8,128)} %get-tuple-element.292) | copy-start | bytes 36868
  54.1 3.5 %copy-start.30 = (f32[4,8,32]{2,1,0:T(8,128)S(1)}, f32[4,8,32]{2,1,0:T(8,128)}, u32[]{:S(2)}) copy-start(f32[4,8,32]{2,1,0:T(8,128)} %slice.1319) | copy-start | bytes 12292
  54.1 3.5 %copy-start.34 = (f32[4,8,32]{2,1,0:T(8,128)S(1)}, f32[4,8,32]{2,1,0:T(8,128)}, u32[]{:S(2)}) copy-start(f32[4,8,32]{2,1,0:T(8,128)} %get-tuple-element.293) | copy-start | bytes 12292
  54.2 3.5 %copy-start.35 = (f32[4,8,32]{2,1,0:T(8,128)S(1)}, f32[4,8,32]{2,1,0:T(8,128)}, u32[]{:S(2)}) copy-start(f32[4,8,32]{2,1,0:T(8,128)} %get-tuple-element.294) | copy-start | bytes 12292
  54.2 3.5 %copy-start.36 = (f32[4,8,32]{2,1,0:T(8,128)S(1)}, f32[4,8,32]{2,1,0:T(8,128)}, u32[]{:S(2)}) copy-start(f32[4,8,32]{2,1,0:T(8,128)} %get-tuple-element.289) | copy-start | bytes 12292
  54.2 3.5 %copy-start.37 = (f32[4,8,32]{2,1,0:T(8,128)S(1)}, f32[4,8,32]{2,1,0:T(8,128)}, u32[]{:S(2)}) copy-start(f32[4,8,32]{2,1,0:T(8,128)} %get-tuple-element.290) | copy-start | bytes 12292
  55.5 2.9 %copy-start.24 = (f32[12,8,32]{2,1,0:T(8,128)S(1)}, f32[12,8,32]{2,1,0:T(8,128)}, u32[]{:S(2)}) copy-start(f32[12,8,32]{2,1,0:T(8,128)} %get-tuple-element.275) | copy-start | bytes 36868
  55.5 2.9 %copy-start.25 = (f32[12,8,32]{2,1,0:T(8,128)S(1)}, f32[12,8,32]{2,1,0:T(8,128)}, u32[]{:S(2)}) copy-start(f32[12,8,32]{2,1,0:T(8,128)} %get-tuple-element.276) | copy-start | bytes 36868
  55.5 2.9 %copy-start.32 = (f32[4,8,32]{2,1,0:T(8,128)S(1)}, f32[4,8,32]{2,1,0:T(8,128)}, u32[]{:S(2)}) copy-start(f32[4,8,32]{2,1,0:T(8,128)} %get-tuple-element.277) | copy-start | bytes 12292
  55.5 2.9 %copy-start.33 = (f32[4,8,32]{2,1,0:T(8,128)S(1)}, f32[4,8,32]{2,1,0:T(8,128)}, u32[]{:S(2)}) copy-start(f32[4,8,32]{2,1,0:T(8,128)} %get-tuple-element.278) | copy-start | bytes 12292
  57.7 0.7 copy-start.11
  57.7 0.7 copy-start.12
  57.7 0.7 copy-start.13
  59.1 1.2 copy-start.40
  59.1 1.2 copy-start.39
  60.5 1.0 copy-start.1
  61.5 1.0 copy-start.7
  61.5 1.2 copy-start.8
  61.5 1.4 copy-start.20
  61.5 1.5 copy-start.21
  81.0 5.0 %copy-start.6 = (f32[8,1,128]{1,0,2:T(8,128)S(1)}, f32[8,1,128]{1,0,2:T(8,128)}, u32[]{:S(2)}) copy-start(f32[8,1,128]{1,0,2:T(8,128)} %slice.1382) | copy-start | bytes 12292
  86.5 0.6 copy-start.38
  171.1 1.0 copy-start.4
Sparse Core Ops, SparseCore 0:
  87.3 78.5 all-gather.3
where the time goes:
time: 181 us; the launch traced here: 180 us
  waiting for transfers between devices  78.7 us (43%)
  local copies, waits for them, and re-layouts  43.2 us (24%)
  other arithmetic  23.2 us (13%)
  blocking collectives  20.1 us (11%)
  between operations  15 us (8%)
    all_gather x1, waiting for transfers between devices, line_pass(): gathered = lax.all_gather(terms[None], mesh_axis, axis=0, tiled=True)  78.7 us
    all_gather x1, blocking collectives, line_pass(): gathered = lax.all_gather(terms[None], mesh_axis, axis=0, tiled=True)  20.1 us
    slice x9, local copies, waits for them, and re-layouts, row_at(): return lax.index_in_dim(member, place, axis, keepdims=False)  12.1 us
    unnamed x99, local copies, waits for them, and re-layouts  9.24 us
    div x12, other arithmetic, local_solve(): inverse = 1.0 / (excess - lower_band - upper_band)  6.03 us
    slice x26, local copies, waits for them, and re-layouts, earlier(): lax.slice_in_dim(values, 0, length - stride, axis=axis)  4.8 us
    add x10, other arithmetic, local_solve(): sources + left_weight * earlier(sources, stride, axis + 1)  4.04 us
  transfers between devices with their start and end apart: 1, of which 1 were waited for; matrix products, arithmetic and copies ran while one was open for 0% of the time, Pallas kernels for 0%

commit v1 on v0

--- a/solution.py
+++ b/solution.py
@@ -92,7 +92,11 @@
         ],
         0,
     )
-    gathered = lax.all_gather(terms[None], mesh_axis, axis=0, tiled=True)
+    content = terms[None]
+    v1 = jnp.stack([content for _ in range(lax.psum(1, axis_name=mesh_axis))])
+    gathered = jnp.concatenate(
+        lax.all_to_all(v1, axis_name=mesh_axis, split_axis=0, concat_axis=0), axis=0
+    )
     head_p, head_u, head_w, tail_p, tail_u, tail_w, tail_kappa, head_wet = (
         gathered[:, k] for k in range(terms.shape[0])
     )

time: 181 us -> 144 us (0.80)
  starting transfers between devices: 0.01 us -> 24 us
  waiting for transfers between devices: 78.7 us -> 55.7 us
  blocking collectives: 20.1 us -> 0 us
  between operations: 15 us -> 1.58 us
  local copies, waits for them, and re-layouts: 43.2 us -> 39.3 us
    all_gather x1 -> x0, waiting for transfers between devices: 78.7 us -> none  [line_pass(): gathered = lax.all_gather(terms[None], mesh_axis, axis=0, tiled=True)]
    all_to_all x0 -> x2, waiting for transfers between devices: none -> 55.7 us  [line_pass(): lax.all_to_all(v1, axis_name=mesh_axis, split_axis=0, concat_axis=0)]
    all_to_all x0 -> x2, starting transfers between devices: none -> 24 us  [line_pass(): lax.all_to_all(v1, axis_name=mesh_axis, split_axis=0, concat_axis=0)]
    all_gather x1 -> x0, blocking collectives: 20.1 us -> none  [line_pass(): gathered = lax.all_gather(terms[None], mesh_axis, axis=0, tiled=True)]
    unnamed x99 -> x69, local copies, waits for them, and re-layouts: 9.24 us -> 13.1 us
    slice x9, local copies, waits for them, and re-layouts: 12.1 us -> 8.9 us  [row_at(): return lax.index_in_dim(member, place, axis, keepdims=False)]
    div x12, other arithmetic: 6.03 us -> 8.79 us  [local_solve(): inverse = 1.0 / (excess - lower_band - upper_band)]
    another operation x0 -> x2, local copies, waits for them, and re-layouts: none -> 1.99 us  [line_pass(): v1 = jnp.stack([content for _ in range(lax.psum(1, axis_name=mesh_axis))])]
  transfers between devices with their start and end apart: 1 -> 2, of which waited for: 1 -> 1; matrix products, arithmetic and copies ran while one was open for 0% -> 9% of each run, Pallas kernels for 0% -> 0%
where the time goes in v1:
time: 144 us; the launch traced here: 143 us
  waiting for transfers between devices  55.7 us (39%)
  local copies, waits for them, and re-layouts  39.3 us (27%)
  starting transfers between devices  24 us (17%)
  other arithmetic  22 us (15%)
  between operations  1.58 us (1%)
    all_to_all x2, waiting for transfers between devices, line_pass(): lax.all_to_all(v1, axis_name=mesh_axis, split_axis=0, concat_axis=0)  55.7 us
    all_to_all x2, starting transfers between devices, line_pass(): lax.all_to_all(v1, axis_name=mesh_axis, split_axis=0, concat_axis=0)  24 us
    unnamed x69, local copies, waits for them, and re-layouts  13.1 us
    slice x9, local copies, waits for them, and re-layouts, row_at(): return lax.index_in_dim(member, place, axis, keepdims=False)  8.9 us
    div x12, other arithmetic, local_solve(): inverse = 1.0 / (excess - lower_band - upper_band)  8.79 us
    slice x26, local copies, waits for them, and re-layouts, earlier(): lax.slice_in_dim(values, 0, length - stride, axis=axis)  4.8 us
    add x10, other arithmetic, local_solve(): sources + left_weight * earlier(sources, stride, axis + 1)  4.06 us
  transfers between devices with their start and end apart: 2, of which 1 were waited for; matrix products, arithmetic and copies ran while one was open for 9% of the time, Pallas kernels for 0%

profile of v1, /device:TPU:1, one launch (start us, length us, event | category | flops | bytes accessed | tf_op | source)
XLA Modules:
  0.0 142.6 jit_solution(13016574147526797801)
XLA Ops:
  0.0 1.0 copy.395
  1.0 1.0 copy.394
  2.1 1.2 copy.393
  3.4 0.9 convert_multiply_fusion
  4.3 1.0 slice_negate_fusion.2
  5.4 0.9 subtract_divide_fusion.11
  6.3 0.8 pad_maximum_fusion.1
  7.1 1.5 %copy.397 = f32[3,8,32,128]{2,1,3,0:T(8,128)S(1)} copy(f32[3,8,32,128]{3,2,1,0:T(8,128)} %pad_maximum_fusion.1) | data formatting | bytes 786432 | tf_op jit(solution)/shard_map/stack | solution.py:73
  8.9 0.8 copy-done.1
  9.8 0.9 copy-done.18
  18.1 0.7 constant_dynamic-update-slice_fusion.1
  18.8 0.9 stack.34
  19.7 1.9 %reshape.62 = f32[16,1,2048]{2,1,0:T(1,128)} reshape(f32[16,1,8,8,32]{4,3,2,1,0:T(8,128)} %stack.34) | data formatting | bytes 262144
  21.6 7.8 %all-to-all-start = ((f32[16,1,2048]{2,1,0:T(1,128)}), f32[16,1,2048]{2,1,0:T(1,128)S(1)}, u32[]{:S(2)}, u32[]{:S(2)}) async-start(f32[16,1,2048]{2,1,0:T(1,128)} %reshape.62), calls=%async_computation | async-start | bytes 262144 | tf_op jit(solution)/shard_map/all_to_all | solution.py:98
  30.4 0.6 copy-done.22
  31.1 1.4 subtract_divide_fusion.3
  33.1 1.4 %subtract_divide_fusion.2 = (f32[8,32,128]{1,0,2:T(8,128)S(1)}, f32[8,32,128]{1,0,2:T(8,128)S(1)}, f32[8,32,128]{1,0,2:T(8,128)S(1)}, f32[8,32,128]{1,0,2:T(8,12...) fusion(f32[8,30,128]{1,0,2:T(8,128)S(1)} %bitcast.192, f32[8,30,128]{1,0,2:T(8,128)S(1)} %get-tuple-element.315, ...), kind=kLoop, calls=%fused_computation.42 | loop fusion | flops 425984 | bytes 1916928 | tf_op jit(solution)/shard_map/div | solution.py:23
  35.1 1.4 subtract_divide_fusion.1
  37.1 1.5 %subtract_divide_fusion = (f32[8,32,128]{1,0,2:T(8,128)S(1)}, f32[8,32,128]{1,0,2:T(8,128)S(1)}, f32[8,32,128]{1,0,2:T(8,128)S(1)}, f32[8,32,128]{1,0,2:T(8,128)...) fusion(f32[8,24,128]{1,0,2:T(8,128)S(1)} %bitcast.194, f32[8,24,128]{1,0,2:T(8,128)S(1)} %get-tuple-element.162, ...), kind=kLoop, calls=%fused_computation.30 | loop fusion | flops 425984 | bytes 1769472 | tf_op jit(solution)/shard_map/div | solution.py:23
  39.2 1.6 %multiply_subtract_fusion = (f32[8,32,128]{1,0,2:T(8,128)}, f32[8,32,128]{1,0,2:T(8,128)}, f32[8,32,128]{1,0,2:T(8,128)}) fusion(f32[8,16,128]{1,0,2:T(8,128)S(1)} %slice.1372, f32[8,16,128]{1,0,2:T(8,128)S(1)} %bitcast.191, f32[8,16,128]{1,0,2:T(8,128)S(1)} %get-tuple-element.158, f32[8,32,128]{1,0,2:T(8,128)S(1)} %get-tuple-element.32, ...), kind=kLoop, calls=%fused_computation.27 | loop fusion | flops 393216 | bytes 1179648 | tf_op jit(solution)/shard_map/sub | solution.py:40
  40.8 1.0 slice.1382
  41.9 1.2 copy.412
  43.4 0.5 broadcast.311
  43.9 0.9 reduce
  46.8 0.5 copy-done.4
  47.5 0.5 multiply_add_fusion.3
  48.5 0.5 copy-done.9
  49.2 0.5 multiply_add_fusion.2
  49.7 0.5 fusion.66
  50.2 0.5 copy-done.11
  50.9 0.6 multiply_add_fusion.1
  52.0 0.5 copy-done.13
  52.7 0.5 multiply_add_fusion
  53.8 0.5 copy-done.15
  54.6 0.8 add_divide_fusion
  55.5 1.1 fusion.78
  56.6 1.2 copy.406
  57.8 1.1 fusion.77
  59.0 1.3 copy.407
  60.3 1.2 fusion.76
  61.4 1.3 copy.408
  62.9 1.2 copy.410
  64.5 1.1 stack.38
  65.6 16.3 %all-to-all-start.1 = ((f32[32,1,8,8,128]{4,3,2,1,0:T(8,128)}), f32[32,1,8,8,128]{4,3,2,1,0:T(8,128)}, u32[]{:S(2)}, u32[]{:S(2)}) async-start(f32[32,1,8,8,128]{4,3,2,1,0:T(8,128)} %stack.38), calls=%async_computation.1 | async-start | bytes 2097152 | tf_op jit(solution)/shard_map/all_to_all | solution.py:98
  81.9 55.7 %all-to-all-done.1 = f32[32,1,8,8,128]{4,3,2,1,0:T(8,128)} async-done(((f32[32,1,8,8,128]{4,3,2,1,0:T(8,128)}), f32[32,1,8,8,128]{4,3,2,1,0:T(8,128)}, u32[]{:S(2)}, u32[]{:S(2)}) %all-to-all-start.1) | async-done | bytes 1048608 | tf_op jit(solution)/shard_map/all_to_all | solution.py:98
  137.6 1.3 copy.426
  140.8 0.5 copy-done.3
  141.8 0.9 copy.417
  (245 shorter events, 17.8 us)
Async XLA Ops:
  2.1 2.2 %copy-start.2 = (bf16[8,32,128]{1,0,2:T(8,128)(2,1)}, bf16[8,32,128]{1,0,2:T(8,128)(2,1)S(1)}, u32[]{:S(2)}) copy-start(bf16[8,32,128]{1,0,2:T(8,128)(2,1)S(1)} %copy.394) | copy-start | bytes 196612
  4.3 2.0 %copy-start.6 = (f32[8,32,128]{1,0,2:T(8,128)}, f32[8,32,128]{1,0,2:T(8,128)S(1)}, u32[]{:S(2)}) copy-start(f32[8,32,128]{1,0,2:T(8,128)S(1)} %get-tuple-element.176) | copy-start | bytes 393220
  4.3 2.0 %copy-start.24 = (f32[8,32,128]{2,1,0:T(8,128)S(1)}, f32[8,32,128]{2,1,0:T(8,128)}, u32[]{:S(2)}) copy-start(f32[8,32,128]{2,1,0:T(8,128)} %param.4) | copy-start | bytes 393220
  8.6 1.0 copy-start.1
  8.6 1.2 copy-start.21
  9.7 1.1 copy-start.18
  9.7 1.2 copy-start.19
  9.7 1.4 copy-start.20
  17.9 11.4 %copy-start = (f32[8,32,128]{1,0,2:T(8,128)S(1)}, f32[8,32,128]{1,0,2:T(8,128)}, u32[]{:S(2)}) copy-start(f32[8,32,128]{1,0,2:T(8,128)} %get-tuple-element.175) | copy-start | bytes 393220
  21.6 21.7 %all-to-all-start = ((f32[16,1,2048]{2,1,0:T(1,128)}), f32[16,1,2048]{2,1,0:T(1,128)S(1)}, u32[]{:S(2)}, u32[]{:S(2)}) async-start(f32[16,1,2048]{2,1,0:T(1,128)} %reshape.62), calls=%async_computation | async-start | bytes 262144 | tf_op jit(solution)/shard_map/all_to_all | solution.py:98
  29.9 1.0 copy-start.22
  29.9 1.2 copy-start.23
  46.3 1.0 copy-start.4
  46.3 1.2 copy-start.5
  48.0 1.0 copy-start.9
  48.0 1.2 copy-start.10
  49.7 1.0 copy-start.11
  49.7 1.2 copy-start.12
  51.5 1.0 copy-start.13
  51.5 1.2 copy-start.14
  53.2 1.0 copy-start.15
  53.2 1.2 copy-start.16
  53.2 1.3 copy-start.17
  59.0 3.7 %copy-start.7 = (f32[8,1,128]{1,0,2:T(8,128)S(1)}, f32[8,1,128]{1,0,2:T(8,128)}, u32[]{:S(2)}) copy-start(f32[8,1,128]{1,0,2:T(8,128)} %get-tuple-element.153) | copy-start | bytes 12292
  61.4 2.8 %copy-start.8 = (f32[8,1,128]{1,0,2:T(8,128)S(1)}, f32[8,1,128]{1,0,2:T(8,128)}, u32[]{:S(2)}) copy-start(f32[8,1,128]{1,0,2:T(8,128)} %get-tuple-element.149) | copy-start | bytes 12292
  65.6 72.0 %all-to-all-start.1 = ((f32[32,1,8,8,128]{4,3,2,1,0:T(8,128)}), f32[32,1,8,8,128]{4,3,2,1,0:T(8,128)}, u32[]{:S(2)}, u32[]{:S(2)}) async-start(f32[32,1,8,8,128]{4,3,2,1,0:T(8,128)} %stack.38), calls=%async_computation.1 | async-start | bytes 2097152 | tf_op jit(solution)/shard_map/all_to_all | solution.py:98
  140.4 1.0 copy-start.3
